TPU v7x, 512 devices: a whole 4x4x16 slice. The times are simulated.
512 devices in a mesh: blk: 32 (over z, core), col: 16 (over y, x).
Axes of the slice: x: 4, y: 4, z: 16, core: 2. Of those that a mesh axis runs over, the one named last changes fastest.
Arguments:
- density: float32 [96, 7, 256, 256], P('blk', None, 'col'), as said below
- band_widths: int32 [96], P('blk'), may hold values from 1 to 3, as said below
Outputs:
- purified: float32 [96, 7, 256, 256], P('blk', None, 'col')
Inputs may be any that keep to these rules, and one draw needn't show every extreme that they name: `band_widths`: each block row keeps between 1 and 3 blocks on each side; 3 is reached in every draw. `density`: diagonal entries of the diagonal blocks lie between 0.05 and 0.95, all other entries are small.
All inputs are finite; a program needn't handle non-finite values.
Results may differ from a plain program's by a relative error of at most 0.00013.
Values sent between devices are 32-bit elements; how exact they have to be, the bound alone decides.
No kernel may reach another device: no remote copies, remote signals or barrier semaphores. Data moves between devices by JAX's collectives and lax.ppermute only.
A program may use at most 64 MiB of HBM per device.

v0:
```python
import jax
import jax.numpy as jnp
from jax import lax
from jax.sharding import PartitionSpec as P

W = 3


def padded(cells, sides, width):
    for axis, dim in sides:
        count = lax.axis_size(axis)
        head = lax.slice_in_dim(cells, 0, width, axis=dim)
        tail = lax.slice_in_dim(cells, cells.shape[dim] - width, cells.shape[dim], axis=dim)
        cells = jnp.concatenate(
            [
                lax.ppermute(tail, axis, [(i, (i + 1) % count) for i in range(count)]),
                cells,
                lax.ppermute(head, axis, [((i + 1) % count, i) for i in range(count)]),
            ],
            axis=dim,
        )
    return cells


def extend(right):
    return padded(right, (("blk", 0),), W)


def contract(extended, shard_rows):
    local_rows = shard_rows.shape[0]
    summed_bands = [None] * (2 * W + 1)
    for inner_band in range(2 * W + 1):
        lowest = max(0, inner_band - W)
        highest = min(2 * W, inner_band + W)
        source_low = lowest - inner_band + W
        source_high = highest - inner_band + W
        block_terms = jnp.einsum(
            "ibcs,isr->ibcr",
            extended[inner_band : inner_band + local_rows, source_low : source_high + 1],
            shard_rows[:, inner_band],
            precision=lax.Precision.HIGHEST,
        )
        for right_band in range(lowest, highest + 1):
            term = block_terms[:, right_band - lowest]
            summed_bands[right_band] = (
                term if summed_bands[right_band] is None else summed_bands[right_band] + term
            )
    return jnp.stack(summed_bands, axis=1)


def gather_columns(cells):
    count = lax.axis_size("col")
    copies = jnp.tile(cells, (1, 1, count, 1))
    return lax.all_to_all(copies, "col", 2, 2, tiled=True)


def on_device(density, band_widths):
    offsets = jnp.abs(jnp.arange(2 * W + 1, dtype=jnp.int32) - W)
    pattern = (offsets[None, :] <= band_widths[:, None]).astype(jnp.float32)[:, :, None, None]
    current = density * pattern
    for purify_step in range(2):
        gathered = gather_columns(current)
        square = contract(extend(current), gathered) * pattern
        third_power = contract(extend(square), gathered) * pattern
        current = 3.0 * square - 2.0 * third_power
    return current


def solution(mesh):
    in_specs = (P("blk", None, "col", None), P("blk"))
    out_specs = P("blk", None, "col", None)
    return jax.shard_map(
        on_device, mesh=mesh, in_specs=in_specs, out_specs=out_specs, check_vma=False
    )
```

profile of v0, /device:TPU:97, one launch (start us, length us, event | category | flops | bytes accessed | tf_op | source)
XLA Modules:
  0.0 297.1 jit_solution(9465738125793480264)
XLA Ops:
  0.0 0.7 compare_convert_fusion
  0.7 1.1 broadcast_multiply_fusion.2
  1.8 0.2 copy.21
  2.0 3.2 %tile.8 = f32[3,7,16,16,256]{4,1,0,3,2:T(8,128)} broadcast(f32[3,7,16,256]{3,1,0,2:T(8,128)S(1)} %copy.21), dimensions={0,1,3,4} | broadcast | bytes 5849088 | tf_op jit(solution)/shard_map/tile | solution.py:53
  5.3 6.8 %all-to-all-start = ((f32[3,7,256,256]{3,1,0,2:T(8,128)}), f32[3,7,256,256]{3,1,0,2:T(8,128)}, u32[]{:S(2)}, u32[]{:S(2)}) async-start(f32[3,7,256,256]{3,1,0,2:T(8,128)} %bitcast.112), calls=%async_computation | async-start | bytes 12582912 | tf_op jit(solution)/shard_map/all_to_all | solution.py:54
  12.1 3.7 %collective-permute-start = (f32[3,7,16,256]{3,2,1,0:T(8,128)S(1)}, f32[3,7,16,256]{3,2,1,0:T(8,128)}, u32[]{:S(2)}, u32[]{:S(2)}) collective-permute-start(f32[3,7,16,256]{3,2,1,0:T(8,128)S(1)} %broadcast_multiply_fusion.2), channel_id=1, source_target_pairs={{0,16},{16,32},{32,48},{48,64},{64,80},{80,96},{96,112},{112,128},... | collective-permute-start | bytes 1032200 | tf_op jit(solution)/shard_map/ppermute | solution.py:16
  15.8 88.6 %all-to-all-done = f32[3,7,256,256]{3,1,0,2:T(8,128)} async-done(((f32[3,7,256,256]{3,1,0,2:T(8,128)}), f32[3,7,256,256]{3,1,0,2:T(8,128)}, u32[]{:S(2)}, u32[]{:S(2)}) %all-to-all-start) | async-done | bytes 5505056 | tf_op jit(solution)/shard_map/all_to_all | solution.py:54
  104.4 20.6 %fusion.45 = (f32[3,1,256,256]{3,1,0,2:T(1,128)S(1)}, f32[3,1,256,256]{3,1,0,2:T(1,128)}, f32[3,1,256,256]{3,1,0,2:T(1,128)S(1)}, f32[3,1,256,256]{3,1,0,2:T(1,1...) fusion(f32[3,7,256,256]{3,1,0,2:T(8,128)} %all-to-all-done), kind=kLoop, calls=%fused_computation.222 | loop fusion | bytes 11010048 | tf_op jit(solution)/shard_map/slice | solution.py:40
  125.0 1.8 fusion.7
  126.8 1.5 fusion.5
  128.3 1.5 fusion.1
  129.9 1.8 fusion.3
  131.7 1.5 fusion.9
  133.3 1.5 fusion.11
  134.8 1.5 fusion.13
  136.6 4.6 %collective-permute-start.2 = (f32[3,7,16,256]{3,2,1,0:T(8,128)S(1)}, f32[3,7,16,256]{3,2,1,0:T(8,128)S(1)}, u32[]{:S(2)}, u32[]{:S(2)}) collective-permute-start(f32[3,7,16,256]{3,2,1,0:T(8,128)S(1)} %broadcast_multiply_fusion.1), channel_id=1, source_target_pairs={{0,16},{16,32},{32,48},{48,64},{64,80},{80,96},{96,112},{112,128},... | collective-permute-start | bytes 1032200 | tf_op jit(solution)/shard_map/ppermute | solution.py:16
  141.2 0.6 fusion.6
  141.8 3.6 %collective-permute-done.2 = f32[3,7,16,256]{3,2,1,0:T(8,128)S(1)} collective-permute-done((f32[3,7,16,256]{3,2,1,0:T(8,128)S(1)}, f32[3,7,16,256]{3,2,1,0:T(8,128)S(1)}, u32[]{:S(2)}, u32[]{:S(2)}) %collective-permute-start.2) | collective-permute-done | bytes 344096 | tf_op jit(solution)/shard_map/ppermute | solution.py:16
  145.4 0.6 fusion
  146.0 0.6 fusion.4
  146.6 0.6 fusion.2
  147.2 1.9 collective-permute-done.3
  149.1 0.6 fusion.8
  149.7 0.6 fusion.10
  150.3 0.6 fusion.12
  151.4 3.2 %tile.20 = f32[3,7,16,16,256]{4,1,0,3,2:T(8,128)} broadcast(f32[3,7,16,256]{3,1,0,2:T(8,128)S(1)} %copy.29), dimensions={0,1,3,4} | broadcast | bytes 5849088 | tf_op jit(solution)/shard_map/tile | solution.py:53
  154.6 5.4 %all-to-all-start.1 = ((f32[3,7,256,256]{3,1,0,2:T(8,128)}), f32[3,7,256,256]{3,1,0,2:T(8,128)}, u32[]{:S(2)}, u32[]{:S(2)}) async-start(f32[3,7,256,256]{3,1,0,2:T(8,128)} %bitcast.113), calls=%async_computation.1 | async-start | bytes 12582912 | tf_op jit(solution)/shard_map/all_to_all | solution.py:54
  160.1 2.9 collective-permute-start.4
  163.0 89.2 %all-to-all-done.1 = f32[3,7,256,256]{3,1,0,2:T(8,128)} async-done(((f32[3,7,256,256]{3,1,0,2:T(8,128)}), f32[3,7,256,256]{3,1,0,2:T(8,128)}, u32[]{:S(2)}, u32[]{:S(2)}) %all-to-all-start.1) | async-done | bytes 5505056 | tf_op jit(solution)/shard_map/all_to_all | solution.py:54
  252.2 20.6 %fusion.44 = (f32[3,1,256,256]{3,1,0,2:T(1,128)S(1)}, f32[3,1,256,256]{3,1,0,2:T(1,128)}, f32[3,1,256,256]{3,1,0,2:T(1,128)S(1)}, f32[3,1,256,256]{3,1,0,2:T(1,1...) fusion(f32[3,7,256,256]{3,1,0,2:T(8,128)} %all-to-all-done.1), kind=kLoop, calls=%fused_computation.221 | loop fusion | bytes 11010048 | tf_op jit(solution)/shard_map/slice | solution.py:40
  272.8 1.8 fusion.21
  274.6 1.6 fusion.15
  276.2 1.5 fusion.19
  277.7 1.8 fusion.17
  279.6 1.5 fusion.23
  281.1 1.5 fusion.25
  282.7 1.5 fusion.27
  284.4 1.9 collective-permute-start.6
  286.4 0.6 fusion.20
  287.0 3.6 %collective-permute-done.6 = f32[3,7,16,256]{3,2,1,0:T(8,128)S(1)} collective-permute-done((f32[3,7,16,256]{3,2,1,0:T(8,128)S(1)}, f32[3,7,16,256]{3,2,1,0:T(8,128)S(1)}, u32[]{:S(2)}, u32[]{:S(2)}) %collective-permute-start.6) | collective-permute-done | bytes 344096 | tf_op jit(solution)/shard_map/ppermute | solution.py:16
  290.6 0.6 fusion.14
  291.2 0.6 fusion.18
  291.8 0.6 fusion.16
  292.4 1.9 collective-permute-done.7
  294.3 0.6 fusion.22
  294.9 0.6 fusion.24
  295.5 0.6 fusion.26
  296.2 0.9 multiply_subtract_fusion
  (53 shorter events, 1.2 us)
Async XLA Ops:
  5.3 99.1 %all-to-all-start = ((f32[3,7,256,256]{3,1,0,2:T(8,128)}), f32[3,7,256,256]{3,1,0,2:T(8,128)}, u32[]{:S(2)}, u32[]{:S(2)}) async-start(f32[3,7,256,256]{3,1,0,2:T(8,128)} %bitcast.112), calls=%async_computation | async-start | bytes 12582912 | tf_op jit(solution)/shard_map/all_to_all | solution.py:54
  12.1 114.7 %collective-permute-start = (f32[3,7,16,256]{3,2,1,0:T(8,128)S(1)}, f32[3,7,16,256]{3,2,1,0:T(8,128)}, u32[]{:S(2)}, u32[]{:S(2)}) collective-permute-start(f32[3,7,16,256]{3,2,1,0:T(8,128)S(1)} %broadcast_multiply_fusion.2), channel_id=1, source_target_pairs={{0,16},{16,32},{32,48},{48,64},{64,80},{80,96},{96,112},{112,128},... | collective-permute-start | bytes 1032200 | tf_op jit(solution)/shard_map/ppermute | solution.py:16
  15.8 116.0 %collective-permute-start.1 = (f32[3,7,16,256]{3,2,1,0:T(8,128)S(1)}, f32[3,7,16,256]{3,2,1,0:T(8,128)}, u32[]{:S(2)}, u32[]{:S(2)}) collective-permute-start(f32[3,7,16,256]{3,2,1,0:T(8,128)S(1)} %broadcast_multiply_fusion.2), channel_id=1, source_target_pairs={{16,0},{32,16},{48,32},{64,48},{80,64},{96,80},{112,96},{128,112},... | collective-permute-start | bytes 1032200 | tf_op jit(solution)/shard_map/ppermute | solution.py:18
  125.0 8.3 %copy-start.2 = (f32[3,1,256,256]{3,1,0,2:T(1,128)S(1)}, f32[3,1,256,256]{3,1,0,2:T(1,128)}, u32[]{:S(2)}) copy-start(f32[3,1,256,256]{3,1,0,2:T(1,128)} %get-tuple-element.13) | copy-start | bytes 2359300
  126.8 14.4 %copy-start = (f32[3,1,256,256]{3,1,0,2:T(1,128)S(1)}, f32[3,1,256,256]{3,1,0,2:T(1,128)}, u32[]{:S(2)}) copy-start(f32[3,1,256,256]{3,1,0,2:T(1,128)} %get-tuple-element.15) | copy-start | bytes 2359300
  131.7 14.9 %copy-start.4 = (f32[3,1,256,256]{3,1,0,2:T(1,128)S(1)}, f32[3,1,256,256]{3,1,0,2:T(1,128)}, u32[]{:S(2)}) copy-start(f32[3,1,256,256]{3,1,0,2:T(1,128)} %get-tuple-element.17) | copy-start | bytes 2359300
  136.6 8.8 %collective-permute-start.2 = (f32[3,7,16,256]{3,2,1,0:T(8,128)S(1)}, f32[3,7,16,256]{3,2,1,0:T(8,128)S(1)}, u32[]{:S(2)}, u32[]{:S(2)}) collective-permute-start(f32[3,7,16,256]{3,2,1,0:T(8,128)S(1)} %broadcast_multiply_fusion.1), channel_id=1, source_target_pairs={{0,16},{16,32},{32,48},{48,64},{64,80},{80,96},{96,112},{112,128},... | collective-permute-start | bytes 1032200 | tf_op jit(solution)/shard_map/ppermute | solution.py:16
  141.2 7.9 %collective-permute-start.3 = (f32[3,7,16,256]{3,2,1,0:T(8,128)S(1)}, f32[3,7,16,256]{3,2,1,0:T(8,128)S(1)}, u32[]{:S(2)}, u32[]{:S(2)}) collective-permute-start(f32[3,7,16,256]{3,2,1,0:T(8,128)S(1)} %broadcast_multiply_fusion.1), channel_id=1, source_target_pairs={{16,0},{32,16},{48,32},{64,48},{80,64},{96,80},{112,96},{128,112},... | collective-permute-start | bytes 1032200 | tf_op jit(solution)/shard_map/ppermute | solution.py:18
  154.6 97.6 %all-to-all-start.1 = ((f32[3,7,256,256]{3,1,0,2:T(8,128)}), f32[3,7,256,256]{3,1,0,2:T(8,128)}, u32[]{:S(2)}, u32[]{:S(2)}) async-start(f32[3,7,256,256]{3,1,0,2:T(8,128)} %bitcast.113), calls=%async_computation.1 | async-start | bytes 12582912 | tf_op jit(solution)/shard_map/all_to_all | solution.py:54
  160.0 119.5 %collective-permute-start.5 = (f32[3,7,16,256]{3,2,1,0:T(8,128)S(1)}, f32[3,7,16,256]{3,2,1,0:T(8,128)}, u32[]{:S(2)}, u32[]{:S(2)}) collective-permute-start(f32[3,7,16,256]{3,2,1,0:T(8,128)S(1)} %multiply_subtract_fusion.1), channel_id=1, source_target_pairs={{16,0},{32,16},{48,32},{64,48},{80,64},{96,80},{112,96},{128,112},... | collective-permute-start | bytes 1032200 | tf_op jit(solution)/shard_map/ppermute | solution.py:18
  160.1 114.5 %collective-permute-start.4 = (f32[3,7,16,256]{3,2,1,0:T(8,128)S(1)}, f32[3,7,16,256]{3,2,1,0:T(8,128)}, u32[]{:S(2)}, u32[]{:S(2)}) collective-permute-start(f32[3,7,16,256]{3,2,1,0:T(8,128)S(1)} %multiply_subtract_fusion.1), channel_id=1, source_target_pairs={{0,16},{16,32},{32,48},{48,64},{64,80},{80,96},{96,112},{112,128},... | collective-permute-start | bytes 1032200 | tf_op jit(solution)/shard_map/ppermute | solution.py:16
  272.8 8.3 %copy-start.3 = (f32[3,1,256,256]{3,1,0,2:T(1,128)S(1)}, f32[3,1,256,256]{3,1,0,2:T(1,128)}, u32[]{:S(2)}) copy-start(f32[3,1,256,256]{3,1,0,2:T(1,128)} %get-tuple-element.6) | copy-start | bytes 2359300
  274.6 11.8 %copy-start.1 = (f32[3,1,256,256]{3,1,0,2:T(1,128)S(1)}, f32[3,1,256,256]{3,1,0,2:T(1,128)}, u32[]{:S(2)}) copy-start(f32[3,1,256,256]{3,1,0,2:T(1,128)} %get-tuple-element.8) | copy-start | bytes 2359300
  279.5 12.2 %copy-start.5 = (f32[3,1,256,256]{3,1,0,2:T(1,128)S(1)}, f32[3,1,256,256]{3,1,0,2:T(1,128)}, u32[]{:S(2)}) copy-start(f32[3,1,256,256]{3,1,0,2:T(1,128)} %get-tuple-element.10) | copy-start | bytes 2359300
  284.4 6.1 %collective-permute-start.6 = (f32[3,7,16,256]{3,2,1,0:T(8,128)S(1)}, f32[3,7,16,256]{3,2,1,0:T(8,128)S(1)}, u32[]{:S(2)}, u32[]{:S(2)}) collective-permute-start(f32[3,7,16,256]{3,2,1,0:T(8,128)S(1)} %broadcast_multiply_fusion), channel_id=1, source_target_pairs={{0,16},{16,32},{32,48},{48,64},{64,80},{80,96},{96,112},{112,128},... | collective-permute-start | bytes 1032200 | tf_op jit(solution)/shard_map/ppermute | solution.py:16
  286.4 7.9 %collective-permute-start.7 = (f32[3,7,16,256]{3,2,1,0:T(8,128)S(1)}, f32[3,7,16,256]{3,2,1,0:T(8,128)S(1)}, u32[]{:S(2)}, u32[]{:S(2)}) collective-permute-start(f32[3,7,16,256]{3,2,1,0:T(8,128)S(1)} %broadcast_multiply_fusion), channel_id=1, source_target_pairs={{16,0},{32,16},{48,32},{64,48},{80,64},{96,80},{112,96},{128,112},... | collective-permute-start | bytes 1032200 | tf_op jit(solution)/shard_map/ppermute | solution.py:18
where the time goes:
time: 298 us; the launch traced here: 297 us
  waiting for transfers between devices  189 us (63%)
  local copies, waits for them, and re-layouts  48.1 us (16%)
  matrix products  30.8 us (10%)
  starting transfers between devices  25.4 us (9%)
  other arithmetic  3.53 us (1%)
    all_to_all x2, waiting for transfers between devices, gather_columns(): return lax.all_to_all(copies, 'col', 2, 2, tiled=True)  178 us
    slice x2, local copies, waits for them, and re-layouts, contract(): shard_rows[:, inner_band]  41.2 us
    dot_general x28, matrix products, contract(): jnp.einsum('ibcs,isr->ibcr', extended[inner_band:inner_band + local_rows,...  30.8 us
    ppermute x4, starting transfers between devices, padded(): lax.ppermute(tail, axis, [(i, (i + 1) % count) for i in range(count)])  13.2 us
    all_to_all x2, starting transfers between devices, gather_columns(): return lax.all_to_all(copies, 'col', 2, 2, tiled=True)  12.2 us
    ppermute x4, waiting for transfers between devices, padded(): lax.ppermute(tail, axis, [(i, (i + 1) % count) for i in range(count)])  7.2 us
    another operation x2, local copies, waits for them, and re-layouts, gather_columns(): copies = jnp.tile(cells, (1, 1, count, 1))  6.47 us
  transfers between devices with their start and end apart: 10, of which 6 were waited for; matrix products, arithmetic and copies ran while one was open for 20% of the time, Pallas kernels for 0%

commit v1 on v0

--- a/solution.py
+++ b/solution.py
@@ -4,6 +4,15 @@
 from jax.sharding import PartitionSpec as P
 
 W = 3
+_step_on_frame = lambda local_array, named_axis, dim_i, in_dim: jnp.concatenate(
+    lax.all_to_all(
+        jnp.stack(jnp.split(local_array, lax.axis_size(named_axis), axis=dim_i), axis=0),
+        axis_name=named_axis,
+        split_axis=0,
+        concat_axis=0,
+    ),
+    axis=in_dim,
+)
 
 
 def padded(cells, sides, width):
@@ -51,7 +60,7 @@
 def gather_columns(cells):
     count = lax.axis_size("col")
     copies = jnp.tile(cells, (1, 1, count, 1))
-    return lax.all_to_all(copies, "col", 2, 2, tiled=True)
+    return _step_on_frame(copies, "col", 2, 2)
 
 
 def on_device(density, band_widths):

time: 298 us -> 245 us (0.82)
  waiting for transfers between devices: 189 us -> 167 us
  local copies, waits for them, and re-layouts: 48.1 us -> 32.5 us
  matrix products: 30.8 us -> 16.7 us
    slice x2 -> x0, local copies, waits for them, and re-layouts: 41.2 us -> none  [contract(): shard_rows[:, inner_band]]
    unnamed x12 -> x30, local copies, waits for them, and re-layouts: 0.02 us -> 23.2 us
    all_to_all x2, waiting for transfers between devices: 178 us -> 156 us  [lax.all_to_all(jnp.stack(jnp.split(local_array, lax.axis_size(named_axis)...]
    dot_general x28, matrix products: 30.8 us -> 16.7 us  [contract(): jnp.einsum('ibcs,isr->ibcr', extended[inner_band:inner_band + local_rows,...]
    reshape x0 -> x2, local copies, waits for them, and re-layouts: none -> 6.36 us  [jnp.concatenate(lax.all_to_all(jnp.stack(jnp.split(local_array, lax.axis_...]
    another operation x2, local copies, waits for them, and re-layouts: 6.47 us -> 1.38 us  [gather_columns(): copies = jnp.tile(cells, (1, 1, count, 1))]
  transfers between devices with their start and end apart: 10 -> 10, of which waited for: 6 -> 6; matrix products, arithmetic and copies ran while one was open for 20% -> 7% of each run, Pallas kernels for 0% -> 0%
where the time goes in v1:
time: 245 us; the launch traced here: 244 us
  waiting for transfers between devices  167 us (68%)
  local copies, waits for them, and re-layouts  32.5 us (13%)
  starting transfers between devices  24.1 us (10%)
  matrix products  16.7 us (7%)
  other arithmetic  3.53 us (1%)
    all_to_all x2, waiting for transfers between devices, lax.all_to_all(jnp.stack(jnp.split(local_array, lax.axis_size(named_axis)...  156 us
    unnamed x30, local copies, waits for them, and re-layouts  23.2 us
    dot_general x28, matrix products, contract(): jnp.einsum('ibcs,isr->ibcr', extended[inner_band:inner_band + local_rows,...  16.7 us
    ppermute x4, starting transfers between devices, padded(): lax.ppermute(tail, axis, [(i, (i + 1) % count) for i in range(count)])  12.1 us
    all_to_all x2, starting transfers between devices, lax.all_to_all(jnp.stack(jnp.split(local_array, lax.axis_size(named_axis)...  12 us
    ppermute x4, waiting for transfers between devices, padded(): lax.ppermute(tail, axis, [(i, (i + 1) % count) for i in range(count)])  7.2 us
    reshape x2, local copies, waits for them, and re-layouts, jnp.concatenate(lax.all_to_all(jnp.stack(jnp.split(local_array, lax.axis_...  6.36 us
  transfers between devices with their start and end apart: 10, of which 6 were waited for; matrix products, arithmetic and copies ran while one was open for 7% of the time, Pallas kernels for 0%

profile of v1, /device:TPU:97, one launch (start us, length us, event | category | flops | bytes accessed | tf_op | source)
XLA Modules:
  0.0 244.2 jit_solution(652374113092071855)
XLA Ops:
  0.7 1.1 broadcast_multiply_fusion.2
  2.5 0.8 fusion.59
  3.3 0.8 fusion.58
  4.1 0.8 fusion.57
  4.8 0.8 fusion.56
  5.6 0.8 fusion.55
  6.4 0.8 fusion.54
  7.1 0.8 fusion.53
  7.9 0.8 fusion.52
  8.7 0.8 fusion.51
  9.5 0.8 fusion.50
  10.3 0.8 fusion.49
  11.0 0.7 fusion.48
  11.8 0.8 fusion.47
  12.6 0.8 fusion.46
  13.3 0.8 fusion.45
  14.1 0.8 fusion.44
  14.9 6.8 %all-to-all-start = ((f32[16,3,7,16,256]{4,3,1,2,0:T(8,128)}), f32[16,3,7,16,256]{4,3,1,2,0:T(8,128)}, u32[]{:S(2)}, u32[]{:S(2)}) async-start(f32[16,3,7,16,256]{4,3,1,2,0:T(8,128)} %fusion.44), calls=%async_computation | async-start | bytes 11010048 | tf_op jit(solution)/shard_map/all_to_all | solution.py:8
  21.7 3.7 %collective-permute-start = (f32[3,7,16,256]{3,2,1,0:T(8,128)S(1)}, f32[3,7,16,256]{3,2,1,0:T(8,128)S(1)}, u32[]{:S(2)}, u32[]{:S(2)}) collective-permute-start(f32[3,7,16,256]{3,2,1,0:T(8,128)S(1)} %broadcast_multiply_fusion.2), channel_id=1, source_target_pairs={{0,16},{16,32},{32,48},{48,64},{64,80},{80,96},{96,112},{112,128},... | collective-permute-start | bytes 1032200 | tf_op jit(solution)/shard_map/ppermute | solution.py:25
  25.4 77.4 %all-to-all-done = f32[16,3,7,16,256]{4,3,1,2,0:T(8,128)} async-done(((f32[16,3,7,16,256]{4,3,1,2,0:T(8,128)}), f32[16,3,7,16,256]{4,3,1,2,0:T(8,128)}, u32[]{:S(2)}, u32[]{:S(2)}) %all-to-all-start) | async-done | bytes 5505056 | tf_op jit(solution)/shard_map/all_to_all | solution.py:8
  102.8 3.2 %copy.36 = f32[3,7,16,16,256]{4,3,2,0,1:T(8,128)S(1)} copy(f32[3,7,16,16,256]{4,3,0,1,2:T(8,128)} %bitcast.17) | data formatting | bytes 11010048 | tf_op jit(solution)/shard_map/reshape | solution.py:7
  110.5 4.6 %collective-permute-start.2 = (f32[3,7,16,256]{3,2,1,0:T(8,128)S(1)}, f32[3,7,16,256]{3,2,1,0:T(8,128)S(1)}, u32[]{:S(2)}, u32[]{:S(2)}) collective-permute-start(f32[3,7,16,256]{3,2,1,0:T(8,128)S(1)} %broadcast_multiply_fusion.1), channel_id=1, source_target_pairs={{0,16},{16,32},{32,48},{48,64},{64,80},{80,96},{96,112},{112,128},... | collective-permute-start | bytes 1032200 | tf_op jit(solution)/shard_map/ppermute | solution.py:25
  115.6 3.6 %collective-permute-done.2 = f32[3,7,16,256]{3,2,1,0:T(8,128)S(1)} collective-permute-done((f32[3,7,16,256]{3,2,1,0:T(8,128)S(1)}, f32[3,7,16,256]{3,2,1,0:T(8,128)S(1)}, u32[]{:S(2)}, u32[]{:S(2)}) %collective-permute-start.2) | collective-permute-done | bytes 344096 | tf_op jit(solution)/shard_map/ppermute | solution.py:25
  121.1 1.9 collective-permute-done.3
  125.7 0.8 fusion.43
  126.5 0.8 fusion.42
  127.3 0.8 fusion.41
  128.0 0.8 fusion.40
  128.8 0.8 fusion.39
  129.6 0.8 fusion.38
  130.3 0.8 fusion.37
  131.1 0.8 fusion.36
  131.9 0.8 fusion.35
  132.7 0.8 fusion.34
  133.5 0.8 fusion.33
  134.3 0.7 fusion.32
  135.0 0.8 fusion.31
  135.8 0.8 fusion.30
  136.5 0.8 fusion.29
  137.3 0.8 fusion.28
  138.1 5.2 %all-to-all-start.1 = ((f32[16,3,7,16,256]{4,3,1,2,0:T(8,128)}), f32[16,3,7,16,256]{4,3,1,2,0:T(8,128)}, u32[]{:S(2)}, u32[]{:S(2)}) async-start(f32[16,3,7,16,256]{4,3,1,2,0:T(8,128)} %fusion.28), calls=%async_computation.1 | async-start | bytes 11010048 | tf_op jit(solution)/shard_map/all_to_all | solution.py:8
  143.3 2.1 collective-permute-start.4
  145.4 78.7 %all-to-all-done.1 = f32[16,3,7,16,256]{4,3,1,2,0:T(8,128)} async-done(((f32[16,3,7,16,256]{4,3,1,2,0:T(8,128)}), f32[16,3,7,16,256]{4,3,1,2,0:T(8,128)}, u32[]{:S(2)}, u32[]{:S(2)}) %all-to-all-start.1) | async-done | bytes 5505056 | tf_op jit(solution)/shard_map/all_to_all | solution.py:8
  224.1 3.2 %copy.38 = f32[3,7,16,16,256]{4,3,2,0,1:T(8,128)S(1)} copy(f32[3,7,16,16,256]{4,3,0,1,2:T(8,128)} %bitcast.64) | data formatting | bytes 11010048 | tf_op jit(solution)/shard_map/reshape | solution.py:7
  231.8 1.7 collective-permute-start.6
  234.1 3.6 %collective-permute-done.6 = f32[3,7,16,256]{3,2,1,0:T(8,128)S(1)} collective-permute-done((f32[3,7,16,256]{3,2,1,0:T(8,128)S(1)}, f32[3,7,16,256]{3,2,1,0:T(8,128)S(1)}, u32[]{:S(2)}, u32[]{:S(2)}) %collective-permute-start.6) | collective-permute-done | bytes 344096 | tf_op jit(solution)/shard_map/ppermute | solution.py:25
  239.5 1.9 collective-permute-done.7
  243.4 0.9 multiply_subtract_fusion
  (73 shorter events, 19.7 us)
Async XLA Ops:
  14.9 87.9 %all-to-all-start = ((f32[16,3,7,16,256]{4,3,1,2,0:T(8,128)}), f32[16,3,7,16,256]{4,3,1,2,0:T(8,128)}, u32[]{:S(2)}, u32[]{:S(2)}) async-start(f32[16,3,7,16,256]{4,3,1,2,0:T(8,128)} %fusion.44), calls=%async_computation | async-start | bytes 11010048 | tf_op jit(solution)/shard_map/all_to_all | solution.py:8
  21.7 84.9 %collective-permute-start = (f32[3,7,16,256]{3,2,1,0:T(8,128)S(1)}, f32[3,7,16,256]{3,2,1,0:T(8,128)S(1)}, u32[]{:S(2)}, u32[]{:S(2)}) collective-permute-start(f32[3,7,16,256]{3,2,1,0:T(8,128)S(1)} %broadcast_multiply_fusion.2), channel_id=1, source_target_pairs={{0,16},{16,32},{32,48},{48,64},{64,80},{80,96},{96,112},{112,128},... | collective-permute-start | bytes 1032200 | tf_op jit(solution)/shard_map/ppermute | solution.py:25
  25.4 83.0 %collective-permute-start.1 = (f32[3,7,16,256]{3,2,1,0:T(8,128)S(1)}, f32[3,7,16,256]{3,2,1,0:T(8,128)S(1)}, u32[]{:S(2)}, u32[]{:S(2)}) collective-permute-start(f32[3,7,16,256]{3,2,1,0:T(8,128)S(1)} %broadcast_multiply_fusion.2), channel_id=1, source_target_pairs={{16,0},{32,16},{48,32},{64,48},{80,64},{96,80},{112,96},{128,112},... | collective-permute-start | bytes 1032200 | tf_op jit(solution)/shard_map/ppermute | solution.py:27
  110.5 8.8 %collective-permute-start.2 = (f32[3,7,16,256]{3,2,1,0:T(8,128)S(1)}, f32[3,7,16,256]{3,2,1,0:T(8,128)S(1)}, u32[]{:S(2)}, u32[]{:S(2)}) collective-permute-start(f32[3,7,16,256]{3,2,1,0:T(8,128)S(1)} %broadcast_multiply_fusion.1), channel_id=1, source_target_pairs={{0,16},{16,32},{32,48},{48,64},{64,80},{80,96},{96,112},{112,128},... | collective-permute-start | bytes 1032200 | tf_op jit(solution)/shard_map/ppermute | solution.py:25
  115.0 7.9 %collective-permute-start.3 = (f32[3,7,16,256]{3,2,1,0:T(8,128)S(1)}, f32[3,7,16,256]{3,2,1,0:T(8,128)S(1)}, u32[]{:S(2)}, u32[]{:S(2)}) collective-permute-start(f32[3,7,16,256]{3,2,1,0:T(8,128)S(1)} %broadcast_multiply_fusion.1), channel_id=1, source_target_pairs={{16,0},{32,16},{48,32},{64,48},{80,64},{96,80},{112,96},{128,112},... | collective-permute-start | bytes 1032200 | tf_op jit(solution)/shard_map/ppermute | solution.py:27
  138.1 86.0 %all-to-all-start.1 = ((f32[16,3,7,16,256]{4,3,1,2,0:T(8,128)}), f32[16,3,7,16,256]{4,3,1,2,0:T(8,128)}, u32[]{:S(2)}, u32[]{:S(2)}) async-start(f32[16,3,7,16,256]{4,3,1,2,0:T(8,128)} %fusion.28), calls=%async_computation.1 | async-start | bytes 11010048 | tf_op jit(solution)/shard_map/all_to_all | solution.py:8
  143.3 84.6 %collective-permute-start.4 = (f32[3,7,16,256]{3,2,1,0:T(8,128)S(1)}, f32[3,7,16,256]{3,2,1,0:T(8,128)S(1)}, u32[]{:S(2)}, u32[]{:S(2)}) collective-permute-start(f32[3,7,16,256]{3,2,1,0:T(8,128)S(1)} %multiply_subtract_fusion.1), channel_id=1, source_target_pairs={{0,16},{16,32},{32,48},{48,64},{64,80},{80,96},{96,112},{112,128},... | collective-permute-start | bytes 1032200 | tf_op jit(solution)/shard_map/ppermute | solution.py:25
  145.4 84.3 %collective-permute-start.5 = (f32[3,7,16,256]{3,2,1,0:T(8,128)S(1)}, f32[3,7,16,256]{3,2,1,0:T(8,128)S(1)}, u32[]{:S(2)}, u32[]{:S(2)}) collective-permute-start(f32[3,7,16,256]{3,2,1,0:T(8,128)S(1)} %multiply_subtract_fusion.1), channel_id=1, source_target_pairs={{16,0},{32,16},{48,32},{64,48},{80,64},{96,80},{112,96},{128,112},... | collective-permute-start | bytes 1032200 | tf_op jit(solution)/shard_map/ppermute | solution.py:27
  231.8 5.9 %collective-permute-start.6 = (f32[3,7,16,256]{3,2,1,0:T(8,128)S(1)}, f32[3,7,16,256]{3,2,1,0:T(8,128)S(1)}, u32[]{:S(2)}, u32[]{:S(2)}) collective-permute-start(f32[3,7,16,256]{3,2,1,0:T(8,128)S(1)} %broadcast_multiply_fusion), channel_id=1, source_target_pairs={{0,16},{16,32},{32,48},{48,64},{64,80},{80,96},{96,112},{112,128},... | collective-permute-start | bytes 1032200 | tf_op jit(solution)/shard_map/ppermute | solution.py:25
  233.5 7.9 %collective-permute-start.7 = (f32[3,7,16,256]{3,2,1,0:T(8,128)S(1)}, f32[3,7,16,256]{3,2,1,0:T(8,128)S(1)}, u32[]{:S(2)}, u32[]{:S(2)}) collective-permute-start(f32[3,7,16,256]{3,2,1,0:T(8,128)S(1)} %broadcast_multiply_fusion), channel_id=1, source_target_pairs={{16,0},{32,16},{48,32},{64,48},{80,64},{96,80},{112,96},{128,112},... | collective-permute-start | bytes 1032200 | tf_op jit(solution)/shard_map/ppermute | solution.py:27
